TPU v7x, 128 devices: a whole 4x4x4 slice. The times are simulated.
128 devices in a mesh: wide: 64 (over x, z, y), narrow: 2 (over core).
Axes of the slice: x: 4, y: 4, z: 4, core: 2. Of those that a mesh axis runs over, the one named last changes fastest.
Arguments:
- features: bfloat16 [16384, 512], P(('wide', 'narrow')), may hold values from -6 to 6
- weight: bfloat16 [512, 512], replicated, may hold values from -0.25 to 0.25
- tile_cols: int32 [128, 2, 48], P('wide', 'narrow'), may hold values from 0 to 63
- tile_count: int32 [128, 2], P('wide', 'narrow'), may hold values from 6 to 48, as said below
- tile_weights: bfloat16 [128, 2, 48, 128, 128], P('wide', 'narrow'), may hold values from 0 to 1, as said below
- cotangent: bfloat16 [16384, 512], P(('wide', 'narrow')), may hold values from -6 to 6
Outputs:
- activated: bfloat16 [16384, 512], P(('wide', 'narrow'))
- grad_features: bfloat16 [16384, 512], P(('wide', 'narrow'))
- grad_weight: float32 [512, 512], replicated
Inputs may be any that keep to these rules, and one draw needn't show every extreme that they name: `tile_count`: live slots of one tile row and residue; the largest equals 48 in every draw. `tile_weights`: edge weights; most entries of a tile are zero.
All inputs are finite; a program needn't handle non-finite values.
Results may differ from a plain program's by a relative error of at most 0.007.
Values may be sent and summed in bfloat16 or wider, within the bound.
No kernel may reach another device: no remote copies, remote signals or barrier semaphores. Data moves between devices by JAX's collectives and lax.ppermute only.
A program may use at most 128 MiB of HBM per device.

v0:
```python
import jax
import jax.numpy as jnp
from jax import lax
from jax.sharding import PartitionSpec as P


def per_device(features, weight, tile_cols, tile_count, tile_weights, cotangent):
    tile = features.shape[0]
    width = features.shape[1]
    copies = tile_cols.shape[0]
    slots = tile_cols.shape[2]
    owners = lax.axis_size("wide")
    columns = tile_cols[:, 0, :]
    counts = tile_count[:, 0]
    tiles = tile_weights[:, 0]
    gathered_features = lax.all_gather(features, "wide", axis=0, tiled=True)
    live = (jnp.arange(slots, dtype=jnp.int32)[None, :] < counts[:, None]).astype(jnp.bfloat16)
    onehot = (columns[..., None] == jnp.arange(owners, dtype=jnp.int32)).astype(
        jnp.bfloat16
    ) * live[..., None]
    dense = jnp.einsum("skj,sktc->stjc", onehot, tiles, preferred_element_type=jnp.float32).reshape(
        copies * tile, owners * tile
    )
    degree = 1.0 + lax.psum(jnp.sum(dense, axis=1), "narrow")
    scale = lax.rsqrt(degree)
    panel = dense.astype(jnp.bfloat16)
    panel_t = (
        jnp.einsum("skj,sktc->jcst", onehot, tiles, preferred_element_type=jnp.float32)
        .reshape(owners * tile, copies * tile)
        .astype(jnp.bfloat16)
    )
    cot_both = lax.all_gather(cotangent, "narrow", axis=0, tiled=True)
    panel, panel_t, scale, cot_both = lax.optimization_barrier((panel, panel_t, scale, cot_both))
    projected = jnp.dot(features, weight, preferred_element_type=jnp.float32).astype(jnp.bfloat16)
    own = lax.axis_index("narrow")
    aggregated = jnp.dot(panel, gathered_features, preferred_element_type=jnp.float32)
    partial_sum = jnp.dot(
        aggregated,
        weight.astype(jnp.float32),
        precision=lax.Precision.HIGHEST,
        preferred_element_type=jnp.float32,
    )
    selector = (jnp.arange(copies, dtype=jnp.int32) == own).astype(jnp.float32)
    self_term = selector[:, None, None] * projected.astype(jnp.float32)[None]
    partial_sum = partial_sum + self_term.reshape(copies * tile, width)
    pair = lax.axis_size("narrow")
    theirs = lax.ppermute(partial_sum, "narrow", [(i, pair - 1 - i) for i in range(pair)])
    preact_both = (partial_sum + theirs) * scale[:, None]
    sig = jax.nn.sigmoid(preact_both)
    cot_both = cot_both.astype(jnp.float32)
    all_grad = (cot_both * sig * (1.0 + preact_both * (1.0 - sig)) * scale[:, None]).astype(
        jnp.bfloat16
    )
    preact = lax.dynamic_slice_in_dim(preact_both, own * tile, tile, 0)
    activated = jax.nn.silu(preact).astype(jnp.bfloat16)
    own_grad = lax.dynamic_slice_in_dim(all_grad, own * tile, tile, 0)
    terms = jnp.dot(panel_t, all_grad, preferred_element_type=jnp.float32).astype(jnp.bfloat16)
    weight_terms = lax.dot_general(
        aggregated,
        all_grad.astype(jnp.float32),
        (((0,), (0,)), ((), ())),
        precision=lax.Precision.HIGHEST,
        preferred_element_type=jnp.float32,
    ) + lax.dot_general(
        features, own_grad, (((0,), (0,)), ((), ())), preferred_element_type=jnp.float32
    )
    rows = width // owners
    high = weight_terms.astype(jnp.bfloat16)
    low = (weight_terms - high.astype(jnp.float32)).astype(jnp.bfloat16)
    payload = jnp.concatenate(
        [
            terms.reshape(owners, tile, width),
            high.reshape(owners, rows, width),
            low.reshape(owners, rows, width),
        ],
        axis=1,
    )
    received = lax.all_to_all(payload, "wide", 0, 0, tiled=True)
    band = jnp.sum(
        received[:, tile : tile + rows].astype(jnp.float32)
        + received[:, tile + rows :].astype(jnp.float32),
        axis=0,
    )
    band = (band + lax.ppermute(band, "narrow", [(i, pair - 1 - i) for i in range(pair)])).astype(
        jnp.bfloat16
    )
    grad_weight = (
        lax.all_to_all(
            jnp.broadcast_to(band[None], (owners, rows, width)), "wide", 0, 0, tiled=True
        )
        .reshape(width, width)
        .astype(jnp.float32)
    )
    gathered_sum = jnp.sum(received[:, :tile].astype(jnp.float32), axis=0)
    message = (gathered_sum + own_grad.astype(jnp.float32)).astype(jnp.bfloat16)
    grad_features = lax.dot_general(
        message, weight, (((1,), (1,)), ((), ())), preferred_element_type=jnp.float32
    ).astype(jnp.bfloat16)
    return (activated, grad_features, grad_weight)


def solution(mesh):
    return jax.shard_map(
        per_device,
        mesh=mesh,
        in_specs=(
            P(("wide", "narrow"), None),
            P(),
            P("wide", "narrow", None),
            P("wide", "narrow"),
            P("wide", "narrow", None, None, None),
            P(("wide", "narrow"), None),
        ),
        out_specs=(P(("wide", "narrow"), None), P(("wide", "narrow"), None), P()),
        check_vma=False,
    )
```

profile of v0, /device:TPU:0, one launch (start us, length us, event | category | flops | bytes accessed | tf_op | source)
XLA Modules:
  0.0 263.9 jit_solution(4746101957128973760)
XLA Ops:
  7.2 0.7 all-gather.2.cloned.1.call-update
  7.9 0.9 compare_convert_fusion.1
  9.1 7.7 %fusion.16 = (bf16[2,64,128,128]{3,1,2,0:T(8,128)(2,1)}, bf16[2,128,64,128]{3,2,1,0:T(8,128)(2,1)}, f32[2,64,128,128]{3,1,2,0:T(8,128)S(1)}) fusion(bf16[2,48,128,128]{3,2,1,0:T(8,128)(2,1)S(1)} %bitcast.55, s32[2,48]{1,0:T(2,128)} %bitcast.60, bf16[2,48]{1,0:T(2,128)(2,1)S(1)} %compare_convert_fusion.1), kind=kOutput, calls=%fused_computation.41 | convolution fusion | flops 205533184 | bytes 19923520 | tf_op jit(solution)/shard_map/skj,sktc->stjc/dot_general | solution.py:21
  16.8 1.1 bitcast_reduce_fusion
  17.8 2.5 psum.7
  20.3 2.2 all_gather.6
  22.5 21.9 %copy_bitcast_fusion = (bf16[8192,256]{0,1:T(8,128)(2,1)}, bf16[256,8192]{1,0:T(8,128)(2,1)}) fusion(bf16[32,8,64,128]{3,2,1,0:T(8,128)(2,1)} %bitcast.57, bf16[32,8,64,128]{3,2,1,0:T(8,128)(2,1)} %bitcast.58), kind=kLoop, calls=%fused_computation.5 | loop fusion | bytes 16777216 | tf_op jit(solution)/shard_map/convert_element_type | solution.py:30
  44.8 47.0 %all-gather.2.cloned.1.call-done = bf16[8192,512]{1,0:T(8,128)(2,1)} async-done(((bf16[128,512]{1,0:T(8,128)(2,1)}), bf16[8192,512]{1,0:T(8,128)(2,1)}) %all-gather.2.cloned.1.call-update) | async-done | bytes 8388624 | tf_op jit(solution)/shard_map/all_gather | solution.py:16
  91.8 7.0 %fusion.19 = f32[256,512]{1,0:T(8,128)S(1)} fusion(bf16[256,8192]{1,0:T(8,128)(2,1)} %get-tuple-element.7, bf16[8192,512]{1,0:T(8,128)(2,1)} %all-gather.2.cloned.1.call-done), kind=kOutput, calls=%fused_computation.42 | convolution fusion | flops 2147483648 | bytes 13107200 | tf_op jit(solution)/shard_map/dot_general | solution.py:36
  98.8 0.6 convolution_add_fusion
  99.7 1.9 collective-permute-done
  101.9 0.6 fusion.20
  102.5 4.6 %convolution_convert_fusion = bf16[8192,512]{1,0:T(8,128)(2,1)S(1)} fusion(bf16[8192,256]{0,1:T(8,128)(2,1)} %get-tuple-element.9, bf16[256,512]{1,0:T(8,128)(2,1)S(1)} %get-tuple-element.11), kind=kOutput, calls=%fused_computation.1 | convolution fusion | flops 2151677952 | bytes 12845056 | tf_op jit(solution)/shard_map/dot_general | solution.py:57
  107.4 0.9 pad_maximum_fusion
  108.4 118.2 %all_to_all.10 = bf16[64,144,512]{2,1,0:T(8,128)(2,1)S(1)} all-to-all(bf16[64,144,512]{2,1,0:T(8,128)(2,1)S(1)} %pad_maximum_fusion), channel_id=1, replica_groups=mesh['wide'=64,'narrow'=2] {'wide'}, dimensions={0} | all-to-all | bytes 18874368 | tf_op jit(solution)/shard_map/all_to_all | solution.py:78
  226.6 3.6 %copy-done.2 = bf16[64,144,512]{2,1,0:T(8,128)(2,1)} copy-done((bf16[64,144,512]{2,1,0:T(8,128)(2,1)}, bf16[64,144,512]{2,1,0:T(8,128)(2,1)S(1)}, u32[]{:S(2)}) %copy-start.2) | copy-done | bytes 9437208
  230.5 0.7 multiply_convert_fusion.1
  231.2 0.4 collective-permute-done.1
  231.6 0.8 broadcast_in_dim.2
  232.5 9.1 %all-to-all-start.1 = ((bf16[64,8,512]{2,1,0:T(8,128)(2,1)}), bf16[64,8,512]{2,1,0:T(8,128)(2,1)}, u32[]{:S(2)}, u32[]{:S(2)}) async-start(bf16[64,8,512]{2,1,0:T(8,128)(2,1)} %broadcast_in_dim.2), calls=%async_computation.1 | async-start | bytes 1048576 | tf_op jit(solution)/shard_map/all_to_all | solution.py:88
  241.6 4.8 %convert_reduce_fusion = f32[128,512]{1,0:T(8,128)S(1)} fusion(bf16[64,144,512]{2,1,0:T(8,128)(2,1)} %copy-done.2), kind=kLoop, calls=%fused_computation | loop fusion | flops 8323072 | bytes 8650752 | tf_op jit(solution)/shard_map/reduce_sum | solution.py:94
  246.5 1.0 convolution_convert_fusion.1
  247.4 7.4 %all-to-all-done.1 = bf16[64,8,512]{2,1,0:T(8,128)(2,1)} async-done(((bf16[64,8,512]{2,1,0:T(8,128)(2,1)}), bf16[64,8,512]{2,1,0:T(8,128)(2,1)}, u32[]{:S(2)}, u32[]{:S(2)}) %all-to-all-start.1) | async-done | bytes 524320 | tf_op jit(solution)/shard_map/all_to_all | solution.py:88
  254.9 2.1 bitcast_convert_fusion.1
  (25 shorter events, 1.9 us)
Async XLA Ops:
  7.2 1.9 copy-start
  7.2 84.6 %all-gather.2.cloned.1.call-start = ((), (), s32[]{:S(2)}) async-start(), calls=%async_computation.2 | async-start | bytes 8519680 | tf_op jit(solution)/shard_map/all_gather | solution.py:16
  16.7 3.6 %copy-start.6 = (bf16[128,512]{1,0:T(8,128)(2,1)S(1)}, bf16[128,512]{1,0:T(8,128)(2,1)}, u32[]{:S(2)}) copy-start(bf16[128,512]{1,0:T(8,128)(2,1)} %param.11) | copy-start | bytes 393220
  22.5 22.0 %copy-start.3 = (bf16[512,512]{1,0:T(8,128)(2,1)S(1)}, bf16[512,512]{1,0:T(8,128)(2,1)}, u32[]{:S(2)}) copy-start(bf16[512,512]{1,0:T(8,128)(2,1)} %param.7) | copy-start | bytes 1572868
  22.5 22.0 %copy-start.5 = (bf16[128,512]{1,0:T(8,128)(2,1)S(1)}, bf16[128,512]{1,0:T(8,128)(2,1)}, u32[]{:S(2)}) copy-start(bf16[128,512]{1,0:T(8,128)(2,1)} %param.6) | copy-start | bytes 393220
  99.3 2.2 collective-permute-start
  108.4 148.7 %copy-start.1 = (bf16[2,1,48,128,128]{4,3,2,1,0:T(8,128)(2,1)S(1)}, bf16[2,1,48,128,128]{4,3,2,1,0:T(8,128)(2,1)}, u32[]{:S(2)}) copy-start(bf16[2,1,48,128,128]{4,3,2,1,0:T(8,128)(2,1)} %param.10) | copy-start | bytes 9437188
  226.6 3.6 %copy-start.2 = (bf16[64,144,512]{2,1,0:T(8,128)(2,1)}, bf16[64,144,512]{2,1,0:T(8,128)(2,1)S(1)}, u32[]{:S(2)}) copy-start(bf16[64,144,512]{2,1,0:T(8,128)(2,1)S(1)} %all_to_all.10) | copy-start | bytes 28311556
  230.4 1.3 collective-permute-start.1
  232.5 22.4 %all-to-all-start.1 = ((bf16[64,8,512]{2,1,0:T(8,128)(2,1)}), bf16[64,8,512]{2,1,0:T(8,128)(2,1)}, u32[]{:S(2)}, u32[]{:S(2)}) async-start(bf16[64,8,512]{2,1,0:T(8,128)(2,1)} %broadcast_in_dim.2), calls=%async_computation.1 | async-start | bytes 1048576 | tf_op jit(solution)/shard_map/all_to_all | solution.py:88
  241.6 4.9 %copy-start.4 = (bf16[512,512]{1,0:T(8,128)(2,1)S(1)}, bf16[512,512]{1,0:T(8,128)(2,1)}, u32[]{:S(2)}) copy-start(bf16[512,512]{1,0:T(8,128)(2,1)} %param.7) | copy-start | bytes 1572868
Sparse Core Ops, SparseCore 0:
  10.9 80.8 all-gather.1
where the time goes:
time: 264 us
  blocking collectives  123 us (47%)
  waiting for transfers between devices  57.4 us (22%)
  local copies, waits for them, and re-layouts  26.7 us (10%)
  matrix products  22 us (8%)
  between operations  14.2 us (5%)
  other arithmetic  11.2 us (4%)
  starting transfers between devices  9.54 us (4%)
    all_to_all x1, blocking collectives, per_device(): received = lax.all_to_all(payload, 'wide', 0, 0, tiled=True)  118 us
    all_gather x1, waiting for transfers between devices, per_device(): gathered_features = lax.all_gather(features, 'wide', axis=0, tiled=True)  47 us
    convert_element_type x1, local copies, waits for them, and re-layouts, per_device(): panel_t = jnp.einsum('skj,sktc->jcst', onehot, tiles, preferred_element_t...  21.9 us
    all_to_all x1, starting transfers between devices, per_device(): lax.all_to_all(jnp.broadcast_to(band[None], (owners, rows, width)), 'wide...  9.11 us
    dot_general x1, matrix products, per_device(): jnp.einsum('skj,sktc->stjc', onehot, tiles, preferred_element_type=jnp.fl...  7.69 us
    all_to_all x1, waiting for transfers between devices, per_device(): lax.all_to_all(jnp.broadcast_to(band[None], (owners, rows, width)), 'wide...  7.43 us
    dot_general x1, matrix products, per_device(): jnp.dot(panel, gathered_features, preferred_element_type=jnp.float32)  6.97 us
  transfers between devices with their start and end apart: 4, of which 4 were waited for; matrix products, arithmetic and copies ran while one was open for 15% of the time, Pallas kernels for 0%

commit v1 on v0

--- a/solution.py
+++ b/solution.py
@@ -13,7 +13,9 @@
     columns = tile_cols[:, 0, :]
     counts = tile_count[:, 0]
     tiles = tile_weights[:, 0]
-    gathered_features = lax.all_gather(features, "wide", axis=0, tiled=True)
+    gathered_features = jnp.concatenate(
+        lax.all_to_all(jnp.stack([features] * lax.axis_size("wide")), "wide", 0, 0), axis=0
+    )
     live = (jnp.arange(slots, dtype=jnp.int32)[None, :] < counts[:, None]).astype(jnp.bfloat16)
     onehot = (columns[..., None] == jnp.arange(owners, dtype=jnp.int32)).astype(
         jnp.bfloat16

time: 264 us -> 311 us (1.18)
  waiting for transfers between devices: 57.4 us -> 85 us
  blocking collectives: 123 us -> 140 us
  between operations: 14.2 us -> 0.79 us
  starting transfers between devices: 9.54 us -> 21.4 us
  local copies, waits for them, and re-layouts: 26.7 us -> 31.6 us
    all_to_all x0 -> x1, waiting for transfers between devices: none -> 75.2 us  [per_device(): lax.all_to_all(jnp.stack([features] * lax.axis_size('wide')), 'wide', 0, 0)]
    all_gather x1 -> x0, waiting for transfers between devices: 47 us -> none  [per_device(): gathered_features = lax.all_gather(features, 'wide', axis=0, tiled=True)]
    all_to_all x1, blocking collectives: 118 us -> 135 us  [per_device(): received = lax.all_to_all(payload, 'wide', 0, 0, tiled=True)]
    all_to_all x0 -> x1, starting transfers between devices: none -> 11.9 us  [per_device(): lax.all_to_all(jnp.stack([features] * lax.axis_size('wide')), 'wide', 0, 0)]
    another operation x0 -> x1, local copies, waits for them, and re-layouts: none -> 5.29 us  [per_device(): jnp.stack([features] * lax.axis_size('wide'))]
  transfers between devices with their start and end apart: 4 -> 4, of which waited for: 4 -> 4; matrix products, arithmetic and copies ran while one was open for 15% -> 12% of each run, Pallas kernels for 0% -> 0%
where the time goes in v1:
time: 311 us
  blocking collectives  140 us (45%)
  waiting for transfers between devices  85 us (27%)
  local copies, waits for them, and re-layouts  31.6 us (10%)
  starting transfers between devices  21.4 us (7%)
  matrix products  21.3 us (7%)
  other arithmetic  10.4 us (3%)
    all_to_all x1, blocking collectives, per_device(): received = lax.all_to_all(payload, 'wide', 0, 0, tiled=True)  135 us
    all_to_all x1, waiting for transfers between devices, per_device(): lax.all_to_all(jnp.stack([features] * lax.axis_size('wide')), 'wide', 0, 0)  75.2 us
    convert_element_type x1, local copies, waits for them, and re-layouts, per_device(): panel_t = jnp.einsum('skj,sktc->jcst', onehot, tiles, preferred_element_t...  21.8 us
    all_to_all x1, starting transfers between devices, per_device(): lax.all_to_all(jnp.stack([features] * lax.axis_size('wide')), 'wide', 0, 0)  11.9 us
    all_to_all x1, starting transfers between devices, per_device(): lax.all_to_all(jnp.broadcast_to(band[None], (owners, rows, width)), 'wide...  9.11 us
    all_to_all x1, waiting for transfers between devices, per_device(): lax.all_to_all(jnp.broadcast_to(band[None], (owners, rows, width)), 'wide...  7.43 us
    dot_general x1, matrix products, per_device(): jnp.einsum('skj,sktc->stjc', onehot, tiles, preferred_element_type=jnp.fl...  6.98 us
    dot_general x1, matrix products, per_device(): jnp.dot(panel, gathered_features, preferred_element_type=jnp.float32)  6.97 us
  transfers between devices with their start and end apart: 4, of which 4 were waited for; matrix products, arithmetic and copies ran while one was open for 12% of the time, Pallas kernels for 0%

profile of v1, /device:TPU:0, one launch (start us, length us, event | category | flops | bytes accessed | tf_op | source)
XLA Modules:
  0.0 310.6 jit_solution(9089028174735625603)
XLA Ops:
  0.6 5.3 %stack.2 = bf16[64,128,512]{2,1,0:T(8,128)(2,1)} broadcast(bf16[128,512]{1,0:T(8,128)(2,1)} %param.6), dimensions={1,2} | broadcast | bytes 8519680 | tf_op jit(solution)/shard_map/stack | solution.py:17
  5.9 11.9 %all-to-all-start = ((bf16[64,128,512]{2,1,0:T(8,128)(2,1)}), bf16[64,128,512]{2,1,0:T(8,128)(2,1)}, u32[]{:S(2)}, u32[]{:S(2)}) async-start(bf16[64,128,512]{2,1,0:T(8,128)(2,1)} %stack.2), calls=%async_computation | async-start | bytes 16777216 | tf_op jit(solution)/shard_map/all_to_all | solution.py:17
  18.0 7.0 %fusion.16 = (bf16[2,64,128,128]{3,1,2,0:T(8,128)(2,1)}, bf16[2,128,64,128]{3,2,1,0:T(8,128)(2,1)}, f32[2,64,128,128]{3,1,2,0:T(8,128)S(1)}) fusion(bf16[2,48,128,128]{3,2,1,0:T(8,128)(2,1)S(1)} %bitcast.56, s32[2,48]{1,0:T(2,128)S(1)} %bitcast.61, bf16[2,48]{1,0:T(2,128)(2,1)S(1)} %compare_convert_fusion.1), kind=kOutput, calls=%fused_computation.41 | convolution fusion | flops 205533184 | bytes 19923520 | tf_op jit(solution)/shard_map/skj,sktc->stjc/dot_general | solution.py:23
  24.9 1.1 bitcast_reduce_fusion
  26.0 2.5 psum.7
  28.5 2.2 all_gather.3
  30.7 21.8 %copy_bitcast_fusion = (bf16[8192,256]{0,1:T(8,128)(2,1)}, bf16[256,8192]{1,0:T(8,128)(2,1)}) fusion(bf16[32,8,64,128]{3,2,1,0:T(8,128)(2,1)} %bitcast.58, bf16[32,8,64,128]{3,2,1,0:T(8,128)(2,1)} %bitcast.59), kind=kLoop, calls=%fused_computation.5 | loop fusion | bytes 16777216 | tf_op jit(solution)/shard_map/convert_element_type | solution.py:32
  52.9 75.2 %all-to-all-done = bf16[64,128,512]{2,1,0:T(8,128)(2,1)} async-done(((bf16[64,128,512]{2,1,0:T(8,128)(2,1)}), bf16[64,128,512]{2,1,0:T(8,128)(2,1)}, u32[]{:S(2)}, u32[]{:S(2)}) %all-to-all-start) | async-done | bytes 8388640 | tf_op jit(solution)/shard_map/all_to_all | solution.py:17
  128.1 7.0 %fusion.19 = f32[256,512]{1,0:T(8,128)S(1)} fusion(bf16[256,8192]{1,0:T(8,128)(2,1)} %get-tuple-element.7, bf16[8192,512]{1,0:T(8,128)(2,1)} %bitcast.8), kind=kOutput, calls=%fused_computation.42 | convolution fusion | flops 2147483648 | bytes 13107200 | tf_op jit(solution)/shard_map/dot_general | solution.py:38
  135.1 0.6 convolution_add_fusion
  136.0 1.9 collective-permute-done
  138.2 0.6 fusion.20
  138.8 4.6 %convolution_convert_fusion = bf16[8192,512]{1,0:T(8,128)(2,1)S(1)} fusion(bf16[8192,256]{0,1:T(8,128)(2,1)} %get-tuple-element.9, bf16[256,512]{1,0:T(8,128)(2,1)S(1)} %get-tuple-element.11), kind=kOutput, calls=%fused_computation.1 | convolution fusion | flops 2151677952 | bytes 12845056 | tf_op jit(solution)/shard_map/dot_general | solution.py:59
  143.8 0.9 pad_maximum_fusion
  144.7 135.5 %all_to_all.15 = bf16[64,144,512]{2,1,0:T(8,128)(2,1)S(1)} all-to-all(bf16[64,144,512]{2,1,0:T(8,128)(2,1)S(1)} %pad_maximum_fusion), channel_id=1, replica_groups=mesh['wide'=64,'narrow'=2] {'wide'}, dimensions={0} | all-to-all | bytes 18874368 | tf_op jit(solution)/shard_map/all_to_all | solution.py:80
  280.2 3.6 %copy-done.2 = bf16[64,144,512]{2,1,0:T(8,128)(2,1)} copy-done((bf16[64,144,512]{2,1,0:T(8,128)(2,1)}, bf16[64,144,512]{2,1,0:T(8,128)(2,1)S(1)}, u32[]{:S(2)}) %copy-start.2) | copy-done | bytes 9437208
  284.0 0.7 multiply_convert_fusion.1
  284.8 0.4 collective-permute-done.1
  285.2 0.8 broadcast_in_dim.2
  286.0 9.1 %all-to-all-start.2 = ((bf16[64,8,512]{2,1,0:T(8,128)(2,1)}), bf16[64,8,512]{2,1,0:T(8,128)(2,1)}, u32[]{:S(2)}, u32[]{:S(2)}) async-start(bf16[64,8,512]{2,1,0:T(8,128)(2,1)} %broadcast_in_dim.2), calls=%async_computation.2 | async-start | bytes 1048576 | tf_op jit(solution)/shard_map/all_to_all | solution.py:90
  295.2 4.8 %convert_reduce_fusion = f32[128,512]{1,0:T(8,128)S(1)} fusion(bf16[64,144,512]{2,1,0:T(8,128)(2,1)} %copy-done.2), kind=kLoop, calls=%fused_computation | loop fusion | flops 8323072 | bytes 8650752 | tf_op jit(solution)/shard_map/reduce_sum | solution.py:96
  300.0 1.0 convolution_convert_fusion.1
  301.0 7.4 %all-to-all-done.2 = bf16[64,8,512]{2,1,0:T(8,128)(2,1)} async-done(((bf16[64,8,512]{2,1,0:T(8,128)(2,1)}), bf16[64,8,512]{2,1,0:T(8,128)(2,1)}, u32[]{:S(2)}, u32[]{:S(2)}) %all-to-all-start.2) | async-done | bytes 524320 | tf_op jit(solution)/shard_map/all_to_all | solution.py:90
  308.4 2.1 bitcast_convert_fusion.1
  (29 shorter events, 1.7 us)
Async XLA Ops:
  0.6 17.3 %copy-start = (bf16[2,1,48,128,128]{4,3,2,1,0:T(8,128)(2,1)S(1)}, bf16[2,1,48,128,128]{4,3,2,1,0:T(8,128)(2,1)}, u32[]{:S(2)}) copy-start(bf16[2,1,48,128,128]{4,3,2,1,0:T(8,128)(2,1)} %param.10) | copy-start | bytes 9437188
  5.9 11.9 %copy-start.8 = (s32[2,1]{0,1:T(1,128)S(1)}, s32[2,1]{0,1:T(1,128)}, u32[]{:S(2)}) copy-start(s32[2,1]{0,1:T(1,128)} %param.9) | copy-start | bytes 28
  5.9 12.0 %copy-start.7 = (s32[2,1,48]{2,1,0:T(1,128)S(1)}, s32[2,1,48]{2,1,0:T(1,128)}, u32[]{:S(2)}) copy-start(s32[2,1,48]{2,1,0:T(1,128)} %param.8) | copy-start | bytes 1156
  5.9 122.2 %all-to-all-start = ((bf16[64,128,512]{2,1,0:T(8,128)(2,1)}), bf16[64,128,512]{2,1,0:T(8,128)(2,1)}, u32[]{:S(2)}, u32[]{:S(2)}) async-start(bf16[64,128,512]{2,1,0:T(8,128)(2,1)} %stack.2), calls=%async_computation | async-start | bytes 16777216 | tf_op jit(solution)/shard_map/all_to_all | solution.py:17
  24.9 3.6 %copy-start.6 = (bf16[128,512]{1,0:T(8,128)(2,1)S(1)}, bf16[128,512]{1,0:T(8,128)(2,1)}, u32[]{:S(2)}) copy-start(bf16[128,512]{1,0:T(8,128)(2,1)} %param.11) | copy-start | bytes 393220
  30.7 21.9 %copy-start.3 = (bf16[512,512]{1,0:T(8,128)(2,1)S(1)}, bf16[512,512]{1,0:T(8,128)(2,1)}, u32[]{:S(2)}) copy-start(bf16[512,512]{1,0:T(8,128)(2,1)} %param.7) | copy-start | bytes 1572868
  30.7 21.9 %copy-start.5 = (bf16[128,512]{1,0:T(8,128)(2,1)S(1)}, bf16[128,512]{1,0:T(8,128)(2,1)}, u32[]{:S(2)}) copy-start(bf16[128,512]{1,0:T(8,128)(2,1)} %param.6) | copy-start | bytes 393220
  135.7 2.2 collective-permute-start
  144.7 165.9 %copy-start.1 = (bf16[2,1,48,128,128]{4,3,2,1,0:T(8,128)(2,1)S(1)}, bf16[2,1,48,128,128]{4,3,2,1,0:T(8,128)(2,1)}, u32[]{:S(2)}) copy-start(bf16[2,1,48,128,128]{4,3,2,1,0:T(8,128)(2,1)} %param.10) | copy-start | bytes 9437188
  280.2 3.6 %copy-start.2 = (bf16[64,144,512]{2,1,0:T(8,128)(2,1)}, bf16[64,144,512]{2,1,0:T(8,128)(2,1)S(1)}, u32[]{:S(2)}) copy-start(bf16[64,144,512]{2,1,0:T(8,128)(2,1)S(1)} %all_to_all.15) | copy-start | bytes 28311556
  283.9 1.3 collective-permute-start.1
  286.0 22.4 %all-to-all-start.2 = ((bf16[64,8,512]{2,1,0:T(8,128)(2,1)}), bf16[64,8,512]{2,1,0:T(8,128)(2,1)}, u32[]{:S(2)}, u32[]{:S(2)}) async-start(bf16[64,8,512]{2,1,0:T(8,128)(2,1)} %broadcast_in_dim.2), calls=%async_computation.2 | async-start | bytes 1048576 | tf_op jit(solution)/shard_map/all_to_all | solution.py:90
  295.2 4.9 %copy-start.4 = (bf16[512,512]{1,0:T(8,128)(2,1)S(1)}, bf16[512,512]{1,0:T(8,128)(2,1)}, u32[]{:S(2)}) copy-start(bf16[512,512]{1,0:T(8,128)(2,1)} %param.7) | copy-start | bytes 1572868
